TPU v7x, 512 devices: a whole 4x8x8 slice. The times are simulated.
512 devices in a mesh: req: 64 (over y, z), tp: 8 (over x, core).
Axes of the slice: x: 4, y: 8, z: 8, core: 2. Of those that a mesh axis runs over, the one named last changes fastest.
Arguments:
- hidden_in: bfloat16 [64, 512, 1024], P(None, 'req', 'tp'), may hold values from -64 to 64
- cache_keys: bfloat16 [64, 512, 1024], P('req', None, 'tp'), may hold values from -250 to 250
- cache_values: bfloat16 [64, 512, 1024], P('req', None, 'tp'), may hold values from -6 to 6
- cache_lengths: int32 [64], replicated, may hold values from 32 to 512, as said below
- owner_order: int32 [64], replicated, may hold values from 0 to 63, as said below
- request_slot: int32 [64], replicated, may hold values from 0 to 63, as said below
- proj_weight: bfloat16 [3, 1024, 1024], P(None, None, 'tp'), may hold values from -0.0625 to 0.0625
- proj_bias: bfloat16 [3, 1024], P(None, 'tp'), may hold values from -1.5 to 1.5
- output_weight: bfloat16 [1024, 1024], P('tp'), may hold values from -0.75 to 0.75
- output_bias: bfloat16 [1024], replicated, may hold values from -2.5 to 2.5
- norm_gains: bfloat16 [2, 1024], replicated, may hold values from 0.5 to 1.5
- norm_biases: bfloat16 [2, 1024], replicated, may hold values from -2.5 to 2.5
- widen_weight: bfloat16 [1024, 4096], P(None, 'tp'), may hold values from -0.1875 to 0.1875
- widen_bias: bfloat16 [4096], P('tp'), may hold values from -2.5 to 2.5
- narrow_weight: bfloat16 [4096, 1024], P('tp'), may hold values from -0.09375 to 0.09375
- narrow_bias: bfloat16 [1024], replicated, may hold values from -2.5 to 2.5
Outputs:
- hidden_out: bfloat16 [64, 512, 1024], P(None, 'req', 'tp')
- new_cache: bfloat16 [2, 64, 512, 1024], P(None, 'req', None, 'tp')
Inputs may be any that keep to these rules, and one draw needn't show every extreme that they name: owner_order is a permutation of the requests; owner slot s lies on index s // 1 of req. request_slot[owner_order[s]] = s for every slot s. `cache_lengths`: given in request order; the longest is exactly 512.
All inputs are finite; a program needn't handle non-finite values.
Results may differ from a plain program's by a relative error of at most 0.014.
Values may be sent and summed in bfloat16 or wider, within the bound.
No kernel may reach another device: no remote copies, remote signals or barrier semaphores. Data moves between devices by JAX's collectives and lax.ppermute only.
A program may use at most 64 MiB of HBM per device.

v0:
```python
import jax
import jax.numpy as jnp
from jax import lax
from jax.sharding import PartitionSpec as P

HD = 64


def layer_norm(values, scale_row, shift_row):
    average = jnp.mean(values, axis=-1, keepdims=True)
    centred = values - average
    spread = jnp.mean(centred * centred, axis=-1, keepdims=True)
    return centred * lax.rsqrt(spread + 1e-05) * scale_row.astype(jnp.float32) + shift_row.astype(
        jnp.float32
    )


def split_heads(rows_block):
    return rows_block.reshape(rows_block.shape[0], -1, HD)


def block_scores(query_heads, keys_block, allowed):
    scores = jnp.einsum(
        "thd,shd->hts", query_heads, split_heads(keys_block), preferred_element_type=jnp.float32
    )
    return jnp.where(allowed[None], scores, -jnp.inf)


def to_rows(factor):
    return jnp.transpose(factor, (1, 0, 2))


def slot_attention(fields):
    query_rows, key_rows, value_rows, slot_keys, slot_values, length = fields
    fresh_len = query_rows.shape[0]
    block_len = min(512, slot_keys.shape[0])
    block_count = slot_keys.shape[0] // block_len
    query_heads = split_heads(query_rows)
    self_mask = jnp.arange(fresh_len)[:, None] >= jnp.arange(fresh_len)[None, :]
    self_scores = block_scores(query_heads, key_rows, self_mask)
    row_top = jnp.max(self_scores, axis=2, keepdims=True)
    raised = jnp.exp(self_scores - row_top)
    row_total = jnp.sum(raised, axis=2, keepdims=True)
    context = jnp.einsum(
        "hts,shd->thd",
        raised.astype(jnp.bfloat16),
        split_heads(value_rows),
        preferred_element_type=jnp.float32,
    )
    positions = jnp.arange(block_len)

    def one_block(number, carry):
        old_top, old_total, running = carry
        begin_at = number * block_len
        allowed = jnp.broadcast_to((begin_at + positions < length)[None, :], (fresh_len, block_len))
        scores = block_scores(query_heads, slot_keys, allowed)
        new_top = jnp.maximum(old_top, jnp.max(scores, axis=2, keepdims=True))
        factor = jnp.exp(old_top - new_top)
        block_raised = jnp.exp(scores - new_top)
        new_total = old_total * factor + jnp.sum(block_raised, axis=2, keepdims=True)
        added = jnp.einsum(
            "hts,shd->thd",
            block_raised.astype(jnp.bfloat16),
            split_heads(slot_values),
            preferred_element_type=jnp.float32,
        )
        return (new_top, new_total, running * to_rows(factor) + added)

    row_top, row_total, context = lax.fori_loop(
        0, block_count, one_block, (row_top, row_total, context)
    )
    context = context / to_rows(row_total)
    return context.reshape(fresh_len, -1).astype(jnp.bfloat16)


def widen_rows(normed, widen_weight, widen_bias):
    widened = jnp.dot(normed, widen_weight, preferred_element_type=jnp.float32) + widen_bias.astype(
        jnp.float32
    )
    return jax.nn.gelu(widened, approximate=False).astype(jnp.bfloat16)


def on_device(
    hidden_in,
    cache_keys,
    cache_values,
    cache_lengths,
    owner_order,
    request_slot,
    proj_weight,
    proj_bias,
    output_weight,
    output_bias,
    norm_gains,
    norm_biases,
    widen_weight,
    widen_bias,
    narrow_weight,
    narrow_bias,
):
    slot_count = cache_keys.shape[0]
    fresh_len = hidden_in.shape[1] * lax.axis_size("req")
    owned_slots = lax.dynamic_slice_in_dim(
        owner_order, lax.axis_index("req") * slot_count, slot_count
    )
    lengths = jnp.take(cache_lengths, owned_slots)
    gathered = lax.all_gather(hidden_in, "tp", axis=2, tiled=True)
    token_rows = lax.all_to_all(
        jnp.take(gathered, owner_order, axis=0), "req", split_axis=0, concat_axis=1, tiled=True
    )
    flat_rows = token_rows.reshape(slot_count * fresh_len, -1)
    projected = (
        jnp.einsum("td,cdf->ctf", flat_rows, proj_weight, preferred_element_type=jnp.float32)
        + proj_bias.astype(jnp.float32)[:, None, :]
    )
    query_rows = (
        (projected[0] * HD ** (-0.5)).astype(jnp.bfloat16).reshape(slot_count, fresh_len, -1)
    )
    key_rows = projected[1].astype(jnp.bfloat16).reshape(slot_count, fresh_len, -1)
    value_rows = projected[2].astype(jnp.bfloat16).reshape(slot_count, fresh_len, -1)
    new_cache = jnp.stack([key_rows, value_rows], axis=0)
    context = lax.map(
        slot_attention, (query_rows, key_rows, value_rows, cache_keys, cache_values, lengths)
    )
    context = context.reshape(slot_count * fresh_len, -1)
    tp_count = lax.axis_size("tp")
    attended = lax.psum(
        jnp.dot(context, output_weight, preferred_element_type=jnp.float32).astype(jnp.bfloat16),
        "tp",
    ).astype(jnp.float32)
    normed = layer_norm(
        flat_rows.astype(jnp.float32) + attended + output_bias.astype(jnp.float32),
        norm_gains[0],
        norm_biases[0],
    ).astype(jnp.bfloat16)
    activated = widen_rows(normed, widen_weight, widen_bias)
    fed_total = lax.psum(
        jnp.dot(activated, narrow_weight, preferred_element_type=jnp.float32).astype(jnp.bfloat16),
        "tp",
    ).astype(jnp.float32)
    updated = layer_norm(
        normed.astype(jnp.float32) + fed_total + narrow_bias.astype(jnp.float32),
        norm_gains[1],
        norm_biases[1],
    ).astype(jnp.bfloat16)
    column_count = updated.shape[1] // tp_count
    updated = lax.dynamic_slice_in_dim(
        updated, lax.axis_index("tp") * column_count, column_count, 1
    )
    returned = lax.all_to_all(
        updated.reshape(slot_count, fresh_len, -1), "req", split_axis=1, concat_axis=0, tiled=True
    )
    hidden_out = jnp.take(returned, request_slot, axis=0)
    return (hidden_out, new_cache)


def solution(mesh):
    in_specs = (
        P(None, "req", "tp"),
        P("req", None, "tp"),
        P("req", None, "tp"),
        P(),
        P(),
        P(),
        P(None, None, "tp"),
        P(None, "tp"),
        P("tp", None),
        P(),
        P(),
        P(),
        P(None, "tp"),
        P("tp"),
        P("tp", None),
        P(),
    )
    out_specs = (P(None, "req", "tp"), P(None, "req", None, "tp"))
    return jax.shard_map(
        on_device, mesh=mesh, in_specs=in_specs, out_specs=out_specs, check_vma=False
    )
```

profile of v0, /device:TPU:8, one launch (start us, length us, event | category | flops | bytes accessed | tf_op | source)
XLA Modules:
  0.0 283.8 jit_solution(11562906684038777593)
XLA Ops:
  7.2 0.0 copy-start
  7.2 0.0 all-gather.2.cloned.1.call-start
  7.2 0.7 all-gather.2.cloned.1.call-update
  7.9 0.7 compare_select_fusion
  8.6 0.7 compare_and_fusion
  9.2 34.1 %all-gather.2.cloned.1.call-done = bf16[64,8,1024]{2,1,0:T(8,128)(2,1)} async-done(((bf16[64,8,128]{2,1,0:T(8,128)(2,1)}), bf16[64,8,1024]{2,1,0:T(8,128)(2,1)}) %all-gather.2.cloned.1.call-update) | async-done | bytes 1048592 | tf_op jit(solution)/shard_map/all_gather | solution.py:107
  43.3 1.8 gather_fusion
  45.1 0.0 copy-start.5
  45.2 0.0 copy-start.13
  45.2 1.1 broadcast_select_fusion
  46.3 13.5 %all-to-all-start = ((bf16[64,8,1024]{2,1,0:T(8,128)(2,1)}), bf16[64,8,1024]{2,1,0:T(8,128)(2,1)S(1)}, u32[]{:S(2)}, u32[]{:S(2)}) async-start(bf16[64,8,1024]{2,1,0:T(8,128)(2,1)} %broadcast_select_fusion), calls=%async_computation | async-start | bytes 2097152 | tf_op jit(solution)/shard_map/all_to_all | solution.py:108
  59.8 0.0 all-reduce.3.cloned.1.call-start
  59.9 0.0 copy-done.5
  59.9 0.1 copy.39
  60.0 0.0 copy-done.13
  60.0 0.6 dynamic_slice.20
  62.6 1.4 copy.36
  64.0 0.8 copy.38
  64.8 0.7 dynamic-slice.5
  66.1 0.1 iota_compare_fusion
  66.2 23.3 %all-to-all-done = bf16[64,8,1024]{2,1,0:T(8,128)(2,1)S(1)} async-done(((bf16[64,8,1024]{2,1,0:T(8,128)(2,1)}), bf16[64,8,1024]{2,1,0:T(8,128)(2,1)S(1)}, u32[]{:S(2)}, u32[]{:S(2)}) %all-to-all-start) | async-done | bytes 1048608 | tf_op jit(solution)/shard_map/all_to_all | solution.py:108
  89.5 0.6 fusion.16
  90.1 0.1 add_bitcast_fusion
  90.3 0.1 copy-done.3
  90.4 0.5 select_reduce_fusion
  90.9 0.6 select_reduce_fusion.1
  91.5 0.6 convolution_bitcast_fusion
  92.1 0.9 fusion.2
  93.0 0.0 copy-start.4
  93.0 0.7 fusion.10
  93.7 0.0 copy-start.12
  93.7 0.0 copy-start.7
  93.7 0.0 copy-start.8
  93.7 0.2 copy-done.4
  93.9 1.5 convolution_convert_fusion
  95.4 0.0 all-reduce.3.cloned.1.call-update
  95.4 0.2 all-reduce.5.cloned.1.call-start
  95.7 0.0 copy-done.7
  95.8 68.0 %all-reduce.3.cloned.1.call-done = bf16[512,1024]{1,0:T(8,128)(2,1)} async-done(((bf16[512,1024]{1,0:T(8,128)(2,1)}), bf16[512,1024]{1,0:T(8,128)(2,1)}) %all-reduce.3.cloned.1.call-update) | async-done | bytes 1048592 | tf_op jit(solution)/shard_map/psum | solution.py:127
  163.8 1.7 fusion.6
  165.5 0.6 multiply_reduce_fusion.1
  166.1 0.6 add_convert_fusion
  166.7 0.0 copy-done
  166.7 0.0 copy-start.10
  166.7 0.0 copy-start.15
  166.7 5.6 %convolution_convert_fusion.1 = bf16[512,1024]{1,0:T(8,128)(2,1)} fusion(bf16[512,1024]{1,0:T(8,128)(2,1)S(1)} %copy-done, bf16[512,1024]{1,0:T(8,128)(2,1)S(1)} %add_convert_fusion, bf16[1024,512]{1,0:T(8,128)(2,1)} %param.28, f32[512]{0:T(512)S(1)} %convert_element_type.122), kind=kOutput, calls=%fused_computation.20 | convolution fusion | flops 1091567616 | bytes 4196352 | tf_op jit(solution)/shard_map/dot_general | solution.py:138
  172.4 0.0 all-reduce.5.cloned.1.call-update
  172.4 0.0 copy-done.10
  172.4 0.1 dynamic-slice.7
  172.5 0.1 dynamic-slice.6
  172.6 72.7 %all-reduce.5.cloned.1.call-done = bf16[512,1024]{1,0:T(8,128)(2,1)} async-done(((bf16[512,1024]{1,0:T(8,128)(2,1)}), bf16[512,1024]{1,0:T(8,128)(2,1)}) %all-reduce.5.cloned.1.call-update) | async-done | bytes 1048592 | tf_op jit(solution)/shard_map/psum | solution.py:137
  245.3 1.7 fusion.1
  247.0 0.6 multiply_reduce_fusion
  247.6 0.1 fusion.66
  247.7 0.2 copy.49
  247.9 0.5 broadcast.99
  248.5 1.4 reduce
  249.9 0.7 reshape.238
  250.6 13.4 %all-to-all-start.1 = ((bf16[64,2,512]{2,1,0:T(2,128)(2,1)}), bf16[64,2,512]{2,1,0:T(2,128)(2,1)S(1)}, u32[]{:S(2)}, u32[]{:S(2)}) async-start(bf16[64,2,512]{2,1,0:T(2,128)(2,1)} %reshape.238), calls=%async_computation.1 | async-start | bytes 262144 | tf_op jit(solution)/shard_map/all_to_all | solution.py:150
  264.0 0.8 copy.42
  264.9 10.8 %all-to-all-done.1 = bf16[64,2,512]{2,1,0:T(2,128)(2,1)S(1)} async-done(((bf16[64,2,512]{2,1,0:T(2,128)(2,1)}), bf16[64,2,512]{2,1,0:T(2,128)(2,1)S(1)}, u32[]{:S(2)}, u32[]{:S(2)}) %all-to-all-start.1) | async-done | bytes 131104 | tf_op jit(solution)/shard_map/all_to_all | solution.py:150
  275.7 0.1 reshape.239
  275.8 0.6 gather_fusion.1
  276.5 0.8 broadcast_select_fusion.1
  (37 shorter events, 0.2 us)
Async XLA Ops:
  7.2 159.5 %copy-start = (bf16[512,1024]{1,0:T(8,128)(2,1)S(1)}, bf16[512,1024]{1,0:T(8,128)(2,1)}, u32[]{:S(2)}) copy-start(bf16[512,1024]{1,0:T(8,128)(2,1)} %param.30) | copy-start | bytes 3145732
  7.2 36.1 %all-gather.2.cloned.1.call-start = ((), (), s32[]{:S(2)}) async-start(), calls=%async_computation.2 | async-start | bytes 1179648 | tf_op jit(solution)/shard_map/all_gather | solution.py:107
  45.1 14.7 %copy-start.5 = (bf16[1,512,128]{2,1,0:T(8,128)(2,1)S(1)}, bf16[1,512,128]{2,1,0:T(8,128)(2,1)}, u32[]{:S(2)}) copy-start(bf16[1,512,128]{2,1,0:T(8,128)(2,1)} %param.18) | copy-start | bytes 393220
  45.2 14.9 %copy-start.13 = (s32[64]{0:T(128)S(1)}, s32[64]{0:T(128)}, u32[]{:S(2)}) copy-start(s32[64]{0:T(128)} %param.20) | copy-start | bytes 772
  46.3 17.7 %copy-start.11 = (bf16[3,128]{1,0:T(4,128)(2,1)S(1)}, bf16[3,128]{1,0:T(4,128)(2,1)}, u32[]{:S(2)}) copy-start(bf16[3,128]{1,0:T(4,128)(2,1)} %param.23) | copy-start | bytes 2308
  46.3 17.7 %copy-start.6 = (bf16[1,512,128]{2,1,0:T(8,128)(2,1)S(1)}, bf16[1,512,128]{2,1,0:T(8,128)(2,1)}, u32[]{:S(2)}) copy-start(bf16[1,512,128]{2,1,0:T(8,128)(2,1)} %param.17) | copy-start | bytes 393220
  46.3 18.5 %copy-start.14 = (s32[64]{0:T(128)S(1)}, s32[64]{0:T(128)}, u32[]{:S(2)}) copy-start(s32[64]{0:T(128)} %param.19) | copy-start | bytes 772
  46.3 43.2 %all-to-all-start = ((bf16[64,8,1024]{2,1,0:T(8,128)(2,1)}), bf16[64,8,1024]{2,1,0:T(8,128)(2,1)S(1)}, u32[]{:S(2)}, u32[]{:S(2)}) async-start(bf16[64,8,1024]{2,1,0:T(8,128)(2,1)} %broadcast_select_fusion), calls=%async_computation | async-start | bytes 2097152 | tf_op jit(solution)/shard_map/all_to_all | solution.py:108
  59.8 103.9 %all-reduce.3.cloned.1.call-start = ((), (), s32[]{:S(2)}) async-start(), calls=%async_computation.3 | async-start | bytes 2097152 | tf_op jit(solution)/shard_map/psum | solution.py:127
  89.5 0.9 copy-start.3
  93.0 1.0 copy-start.4
  93.7 2.0 copy-start.9
  93.7 2.0 copy-start.12
  93.7 2.0 copy-start.7
  93.7 2.0 copy-start.8
  95.4 149.8 %all-reduce.5.cloned.1.call-start = ((), (), s32[]{:S(2)}) async-start(), calls=%async_computation.4 | async-start | bytes 2097152 | tf_op jit(solution)/shard_map/psum | solution.py:137
  163.8 1.7 copy-start.1
  166.7 5.7 %copy-start.10 = (bf16[1024]{0:T(1024)(128)(2,1)S(1)}, bf16[1024]{0:T(1024)(128)(2,1)}, u32[]{:S(2)}) copy-start(bf16[1024]{0:T(1024)(128)(2,1)} %param.31) | copy-start | bytes 6148
  166.7 5.9 %copy-start.15 = (s32[64]{0:T(128)S(1)}, s32[64]{0:T(128)}, u32[]{:S(2)}) copy-start(s32[64]{0:T(128)} %param.21) | copy-start | bytes 772
  245.3 1.7 copy-start.2
  250.6 25.1 %all-to-all-start.1 = ((bf16[64,2,512]{2,1,0:T(2,128)(2,1)}), bf16[64,2,512]{2,1,0:T(2,128)(2,1)S(1)}, u32[]{:S(2)}, u32[]{:S(2)}) async-start(bf16[64,2,512]{2,1,0:T(2,128)(2,1)} %reshape.238), calls=%async_computation.1 | async-start | bytes 262144 | tf_op jit(solution)/shard_map/all_to_all | solution.py:150
Sparse Core Ops, SparseCore 0:
  10.1 33.1 all-gather.1
  95.6 68.1 all-reduce.2
  172.5 72.6 all-reduce.4
where the time goes:
time: 284 us
  waiting for transfers between devices  210 us (74%)
  starting transfers between devices  27.2 us (10%)
  between operations  16.8 us (6%)
  other arithmetic  11.2 us (4%)
  matrix products  10 us (4%)
  local copies, waits for them, and re-layouts  8.95 us (3%)
    psum x1, waiting for transfers between devices, on_device(): lax.psum(jnp.dot(activated, narrow_weight, preferred_element_type=jnp.flo...  72.7 us
    psum x1, waiting for transfers between devices, on_device(): lax.psum(jnp.dot(context, output_weight, preferred_element_type=jnp.float...  68 us
    all_gather x1, waiting for transfers between devices, on_device(): gathered = lax.all_gather(hidden_in, 'tp', axis=2, tiled=True)  34.1 us
    all_to_all x1, waiting for transfers between devices, on_device(): lax.all_to_all(jnp.take(gathered, owner_order, axis=0), 'req', split_axis...  23.3 us
    all_to_all x1, starting transfers between devices, on_device(): lax.all_to_all(jnp.take(gathered, owner_order, axis=0), 'req', split_axis...  13.5 us
    all_to_all x1, starting transfers between devices, on_device(): lax.all_to_all(updated.reshape(slot_count, fresh_len, -1), 'req', split_a...  13.4 us
    all_to_all x1, waiting for transfers between devices, on_device(): lax.all_to_all(updated.reshape(slot_count, fresh_len, -1), 'req', split_a...  10.8 us
  transfers between devices with their start and end apart: 5, of which 5 were waited for; matrix products, arithmetic and copies ran while one was open for 2% of the time, Pallas kernels for 0%

commit v1 on v0

--- a/solution.py
+++ b/solution.py
@@ -4,6 +4,35 @@
 from jax.sharding import PartitionSpec as P
 
 HD = 64
+
+
+def roots_rest(content):
+    x_new = lax.psum(1, axis_name="tp")
+    high = lax.axis_index("tp")
+    side_arr, left_arr, b_now = (x_new, high, content.shape[2])
+    pile = [kk * side_arr if to_i == 2 else kk for to_i, kk in enumerate(content.shape)]
+    current_value = jnp.zeros(pile, content.dtype)
+    mid_arr = lax.dynamic_update_slice_in_dim(current_value, content, left_arr * b_now, axis=2)
+    far_arr = next_value = content
+    for pp in range(1, side_arr // 2 + 1):
+        far_arr = lax.ppermute(
+            far_arr,
+            axis_name="tp",
+            perm=[(to_i, (to_i + 1) % side_arr) for to_i in range(side_arr)],
+        )
+        mid_arr = lax.dynamic_update_slice_in_dim(
+            mid_arr, far_arr, (left_arr - pp) % side_arr * b_now, axis=2
+        )
+        if 2 * pp < side_arr:
+            next_value = lax.ppermute(
+                next_value,
+                axis_name="tp",
+                perm=[(to_i, (to_i - 1) % side_arr) for to_i in range(side_arr)],
+            )
+            mid_arr = lax.dynamic_update_slice_in_dim(
+                mid_arr, next_value, (left_arr + pp) % side_arr * b_now, axis=2
+            )
+    return mid_arr
 
 
 def layer_norm(values, scale_row, shift_row):
@@ -104,7 +133,7 @@
         owner_order, lax.axis_index("req") * slot_count, slot_count
     )
     lengths = jnp.take(cache_lengths, owned_slots)
-    gathered = lax.all_gather(hidden_in, "tp", axis=2, tiled=True)
+    gathered = roots_rest(hidden_in)
     token_rows = lax.all_to_all(
         jnp.take(gathered, owner_order, axis=0), "req", split_axis=0, concat_axis=1, tiled=True
     )

time: 284 us -> 268 us (0.944)
  waiting for transfers between devices: 210 us -> 181 us
  starting transfers between devices: 27.2 us -> 39.2 us
    all_gather x1 -> x0, waiting for transfers between devices: 34.1 us -> none  [on_device(): gathered = lax.all_gather(hidden_in, 'tp', axis=2, tiled=True)]
    ppermute x0 -> x7, waiting for transfers between devices: none -> 10.9 us  [the longest x4 10.9 us: roots_rest(): lax.ppermute(far_arr, axis_name='tp', perm=[(to_i, (to_i + 1) % side_arr)...]
    ppermute x0 -> x7, starting transfers between devices: none -> 8.88 us  [the longest x3 8.85 us: roots_rest(): lax.ppermute(next_value, axis_name='tp', perm=[(to_i, (to_i - 1) % side_a...]
    all_to_all x1, waiting for transfers between devices: 23.3 us -> 19.1 us  [on_device(): lax.all_to_all(jnp.take(gathered, owner_order, axis=0), 'req', split_axis...]
    all_to_all x1, starting transfers between devices: 13.5 us -> 16.7 us  [on_device(): lax.all_to_all(jnp.take(gathered, owner_order, axis=0), 'req', split_axis...]
  transfers between devices with their start and end apart: 5 -> 11, of which waited for: 5 -> 8; matrix products, arithmetic and copies ran while one was open for 2% -> 3% of each run, Pallas kernels for 0% -> 0%
where the time goes in v1:
time: 268 us
  waiting for transfers between devices  181 us (68%)
  starting transfers between devices  39.2 us (15%)
  between operations  17.2 us (6%)
  other arithmetic  11.2 us (4%)
  matrix products  10.1 us (4%)
  local copies, waits for them, and re-layouts  9.01 us (3%)
    psum x1, waiting for transfers between devices, on_device(): lax.psum(jnp.dot(activated, narrow_weight, preferred_element_type=jnp.flo...  72.7 us
    psum x1, waiting for transfers between devices, on_device(): lax.psum(jnp.dot(context, output_weight, preferred_element_type=jnp.float...  67.7 us
    all_to_all x1, waiting for transfers between devices, on_device(): lax.all_to_all(jnp.take(gathered, owner_order, axis=0), 'req', split_axis...  19.1 us
    all_to_all x1, starting transfers between devices, on_device(): lax.all_to_all(jnp.take(gathered, owner_order, axis=0), 'req', split_axis...  16.7 us
    all_to_all x1, starting transfers between devices, on_device(): lax.all_to_all(updated.reshape(slot_count, fresh_len, -1), 'req', split_a...  13.4 us
    ppermute x4, waiting for transfers between devices, roots_rest(): lax.ppermute(far_arr, axis_name='tp', perm=[(to_i, (to_i + 1) % side_arr)...  10.9 us
    all_to_all x1, waiting for transfers between devices, on_device(): lax.all_to_all(updated.reshape(slot_count, fresh_len, -1), 'req', split_a...  10.8 us
    ppermute x3, starting transfers between devices, roots_rest(): lax.ppermute(next_value, axis_name='tp', perm=[(to_i, (to_i - 1) % side_a...  8.85 us
  transfers between devices with their start and end apart: 11, of which 8 were waited for; matrix products, arithmetic and copies ran while one was open for 3% of the time, Pallas kernels for 0%

profile of v1, /device:TPU:8, one launch (start us, length us, event | category | flops | bytes accessed | tf_op | source)
XLA Modules:
  0.0 268.0 jit_solution(16667191690838985019)
XLA Ops:
  7.2 0.0 copy-start
  7.2 0.0 collective-permute-start
  7.2 2.9 %collective-permute-start.1 = (bf16[64,8,128]{2,1,0:T(8,128)(2,1)}, bf16[64,8,128]{2,1,0:T(8,128)(2,1)S(1)}, u32[]{:S(2)}, u32[]{:S(2)}) collective-permute-start(bf16[64,8,128]{2,1,0:T(8,128)(2,1)} %param.16), channel_id=1, source_target_pairs={{0,7},{1,0},{2,1},{3,2},{4,3},{5,4},{6,5},{7,6},{8,15},{9,8},{10,9... | collective-permute-start | bytes 393224 | tf_op jit(solution)/shard_map/ppermute | solution.py:27
  10.1 0.7 compare_select_fusion
  10.8 0.7 compare_and_fusion
  11.6 0.1 broadcast_in_dim.107
  11.7 0.9 constant_dynamic-update-slice_fusion.7
  12.7 0.3 collective-permute-done
  13.0 3.0 %collective-permute-start.3 = (bf16[64,8,128]{2,1,0:T(8,128)(2,1)S(1)}, bf16[64,8,128]{2,1,0:T(8,128)(2,1)S(1)}, u32[]{:S(2)}, u32[]{:S(2)}) collective-permute-start(bf16[64,8,128]{2,1,0:T(8,128)(2,1)S(1)} %collective-permute-done.1), channel_id=1, source_target_pairs={{0,7},{1,0},{2,1},{3,2},{4,3},{5,4},{6,5},{7,6},{8,15},{9,8},{10,9... | collective-permute-start | bytes 393224 | tf_op jit(solution)/shard_map/ppermute | solution.py:27
  16.1 2.5 collective-permute-done.2
  18.6 3.0 %collective-permute-start.5 = (bf16[64,8,128]{2,1,0:T(8,128)(2,1)S(1)}, bf16[64,8,128]{2,1,0:T(8,128)(2,1)S(1)}, u32[]{:S(2)}, u32[]{:S(2)}) collective-permute-start(bf16[64,8,128]{2,1,0:T(8,128)(2,1)S(1)} %collective-permute-done.3), channel_id=1, source_target_pairs={{0,7},{1,0},{2,1},{3,2},{4,3},{5,4},{6,5},{7,6},{8,15},{9,8},{10,9... | collective-permute-start | bytes 393224 | tf_op jit(solution)/shard_map/ppermute | solution.py:27
  21.7 2.5 collective-permute-done.4
  24.3 5.5 %collective-permute-done.6 = bf16[64,8,128]{2,1,0:T(8,128)(2,1)S(1)} collective-permute-done((bf16[64,8,128]{2,1,0:T(8,128)(2,1)S(1)}, bf16[64,8,128]{2,1,0:T(8,128)(2,1)S(1)}, u32[]{:S(2)}, u32[]{:S(2)}) %collective-permute-start.6) | collective-permute-done | bytes 131104 | tf_op jit(solution)/shard_map/ppermute | solution.py:18
  29.9 0.6 gather_fusion
  30.5 0.0 copy-start.5
  30.5 0.0 copy-start.13
  30.5 1.1 broadcast_select_fusion
  31.6 16.7 %all-to-all-start = ((bf16[64,8,1024]{2,1,0:T(8,128)(2,1)}), bf16[64,8,1024]{2,1,0:T(8,128)(2,1)S(1)}, u32[]{:S(2)}, u32[]{:S(2)}) async-start(bf16[64,8,1024]{2,1,0:T(8,128)(2,1)} %broadcast_select_fusion), calls=%async_computation | async-start | bytes 2097152 | tf_op jit(solution)/shard_map/all_to_all | solution.py:137
  48.4 0.0 all-reduce.3.cloned.1.call-start
  48.4 0.1 copy.39
  48.6 0.6 dynamic_slice.20
  51.1 1.4 copy.36
  52.5 0.8 copy.38
  53.3 0.6 dynamic-slice.5
  54.6 0.1 iota_compare_fusion
  54.6 19.1 %all-to-all-done = bf16[64,8,1024]{2,1,0:T(8,128)(2,1)S(1)} async-done(((bf16[64,8,1024]{2,1,0:T(8,128)(2,1)}), bf16[64,8,1024]{2,1,0:T(8,128)(2,1)S(1)}, u32[]{:S(2)}, u32[]{:S(2)}) %all-to-all-start) | async-done | bytes 1048608 | tf_op jit(solution)/shard_map/all_to_all | solution.py:137
  73.7 0.6 fusion.16
  74.3 0.1 add_bitcast_fusion
  74.5 0.1 copy-done.3
  74.6 0.5 select_reduce_fusion
  75.1 0.6 select_reduce_fusion.1
  75.7 0.6 convolution_bitcast_fusion
  76.3 0.9 fusion.2
  77.2 0.0 copy-start.4
  77.2 0.7 fusion.10
  77.9 0.0 copy-start.12
  77.9 0.0 copy-start.7
  77.9 0.0 copy-start.8
  77.9 0.2 copy-done.4
  78.1 1.5 convolution_convert_fusion
  79.6 0.0 all-reduce.3.cloned.1.call-update
  79.6 0.2 all-reduce.5.cloned.1.call-start
  80.0 67.7 %all-reduce.3.cloned.1.call-done = bf16[512,1024]{1,0:T(8,128)(2,1)} async-done(((bf16[512,1024]{1,0:T(8,128)(2,1)}), bf16[512,1024]{1,0:T(8,128)(2,1)}) %all-reduce.3.cloned.1.call-update) | async-done | bytes 1048592 | tf_op jit(solution)/shard_map/psum | solution.py:156
  147.6 1.7 fusion.6
  149.4 0.6 multiply_reduce_fusion.1
  150.0 0.6 add_convert_fusion
  150.6 5.7 %convolution_convert_fusion.1 = bf16[512,1024]{1,0:T(8,128)(2,1)} fusion(bf16[512,1024]{1,0:T(8,128)(2,1)S(1)} %copy-done, bf16[512,1024]{1,0:T(8,128)(2,1)S(1)} %add_convert_fusion, bf16[1024,512]{1,0:T(8,128)(2,1)} %param.28, f32[512]{0:T(512)S(1)} %convert_element_type.122), kind=kOutput, calls=%fused_computation.20 | convolution fusion | flops 1091567616 | bytes 4196352 | tf_op jit(solution)/shard_map/dot_general | solution.py:167
  156.3 0.0 all-reduce.5.cloned.1.call-update
  156.3 0.1 dynamic-slice.7
  156.4 0.1 dynamic-slice.6
  156.5 72.7 %all-reduce.5.cloned.1.call-done = bf16[512,1024]{1,0:T(8,128)(2,1)} async-done(((bf16[512,1024]{1,0:T(8,128)(2,1)}), bf16[512,1024]{1,0:T(8,128)(2,1)}) %all-reduce.5.cloned.1.call-update) | async-done | bytes 1048592 | tf_op jit(solution)/shard_map/psum | solution.py:166
  229.2 1.7 fusion.1
  230.9 0.6 multiply_reduce_fusion
  231.5 0.1 fusion.66
  231.6 0.2 copy.49
  231.8 0.5 broadcast.106
  232.3 1.4 reduce
  233.8 0.7 reshape.238
  234.5 13.4 %all-to-all-start.1 = ((bf16[64,2,512]{2,1,0:T(2,128)(2,1)}), bf16[64,2,512]{2,1,0:T(2,128)(2,1)S(1)}, u32[]{:S(2)}, u32[]{:S(2)}) async-start(bf16[64,2,512]{2,1,0:T(2,128)(2,1)} %reshape.238), calls=%async_computation.1 | async-start | bytes 262144 | tf_op jit(solution)/shard_map/all_to_all | solution.py:179
  247.9 0.8 copy.42
  248.8 10.8 %all-to-all-done.1 = bf16[64,2,512]{2,1,0:T(2,128)(2,1)S(1)} async-done(((bf16[64,2,512]{2,1,0:T(2,128)(2,1)}), bf16[64,2,512]{2,1,0:T(2,128)(2,1)S(1)}, u32[]{:S(2)}, u32[]{:S(2)}) %all-to-all-start.1) | async-done | bytes 131104 | tf_op jit(solution)/shard_map/all_to_all | solution.py:179
  259.6 0.1 reshape.239
  259.7 0.6 gather_fusion.1
  260.4 0.8 broadcast_select_fusion.1
  (57 shorter events, 0.5 us)
Async XLA Ops:
  7.2 143.4 %copy-start = (bf16[512,1024]{1,0:T(8,128)(2,1)S(1)}, bf16[512,1024]{1,0:T(8,128)(2,1)}, u32[]{:S(2)}) copy-start(bf16[512,1024]{1,0:T(8,128)(2,1)} %param.30) | copy-start | bytes 3145732
  7.2 5.8 %collective-permute-start = (bf16[64,8,128]{2,1,0:T(8,128)(2,1)}, bf16[64,8,128]{2,1,0:T(8,128)(2,1)S(1)}, u32[]{:S(2)}, u32[]{:S(2)}) collective-permute-start(bf16[64,8,128]{2,1,0:T(8,128)(2,1)} %param.16), channel_id=1, source_target_pairs={{0,1},{1,2},{2,3},{3,4},{4,5},{5,6},{6,7},{7,0},{8,9},{9,10},{10,1... | collective-permute-start | bytes 393224 | tf_op jit(solution)/shard_map/ppermute | solution.py:18
  7.2 5.8 %collective-permute-start.1 = (bf16[64,8,128]{2,1,0:T(8,128)(2,1)}, bf16[64,8,128]{2,1,0:T(8,128)(2,1)S(1)}, u32[]{:S(2)}, u32[]{:S(2)}) collective-permute-start(bf16[64,8,128]{2,1,0:T(8,128)(2,1)} %param.16), channel_id=1, source_target_pairs={{0,7},{1,0},{2,1},{3,2},{4,3},{5,4},{6,5},{7,6},{8,15},{9,8},{10,9... | collective-permute-start | bytes 393224 | tf_op jit(solution)/shard_map/ppermute | solution.py:27
  13.0 5.6 %collective-permute-start.2 = (bf16[64,8,128]{2,1,0:T(8,128)(2,1)S(1)}, bf16[64,8,128]{2,1,0:T(8,128)(2,1)S(1)}, u32[]{:S(2)}, u32[]{:S(2)}) collective-permute-start(bf16[64,8,128]{2,1,0:T(8,128)(2,1)S(1)} %collective-permute-done), channel_id=1, source_target_pairs={{0,1},{1,2},{2,3},{3,4},{4,5},{5,6},{6,7},{7,0},{8,9},{9,10},{10,1... | collective-permute-start | bytes 393224 | tf_op jit(solution)/shard_map/ppermute | solution.py:18
  13.0 5.6 %collective-permute-start.3 = (bf16[64,8,128]{2,1,0:T(8,128)(2,1)S(1)}, bf16[64,8,128]{2,1,0:T(8,128)(2,1)S(1)}, u32[]{:S(2)}, u32[]{:S(2)}) collective-permute-start(bf16[64,8,128]{2,1,0:T(8,128)(2,1)S(1)} %collective-permute-done.1), channel_id=1, source_target_pairs={{0,7},{1,0},{2,1},{3,2},{4,3},{5,4},{6,5},{7,6},{8,15},{9,8},{10,9... | collective-permute-start | bytes 393224 | tf_op jit(solution)/shard_map/ppermute | solution.py:27
  18.6 5.6 %collective-permute-start.4 = (bf16[64,8,128]{2,1,0:T(8,128)(2,1)S(1)}, bf16[64,8,128]{2,1,0:T(8,128)(2,1)S(1)}, u32[]{:S(2)}, u32[]{:S(2)}) collective-permute-start(bf16[64,8,128]{2,1,0:T(8,128)(2,1)S(1)} %collective-permute-done.2), channel_id=1, source_target_pairs={{0,1},{1,2},{2,3},{3,4},{4,5},{5,6},{6,7},{7,0},{8,9},{9,10},{10,1... | collective-permute-start | bytes 393224 | tf_op jit(solution)/shard_map/ppermute | solution.py:18
  18.6 5.6 %collective-permute-start.5 = (bf16[64,8,128]{2,1,0:T(8,128)(2,1)S(1)}, bf16[64,8,128]{2,1,0:T(8,128)(2,1)S(1)}, u32[]{:S(2)}, u32[]{:S(2)}) collective-permute-start(bf16[64,8,128]{2,1,0:T(8,128)(2,1)S(1)} %collective-permute-done.3), channel_id=1, source_target_pairs={{0,7},{1,0},{2,1},{3,2},{4,3},{5,4},{6,5},{7,6},{8,15},{9,8},{10,9... | collective-permute-start | bytes 393224 | tf_op jit(solution)/shard_map/ppermute | solution.py:27
  24.2 5.6 %collective-permute-start.6 = (bf16[64,8,128]{2,1,0:T(8,128)(2,1)S(1)}, bf16[64,8,128]{2,1,0:T(8,128)(2,1)S(1)}, u32[]{:S(2)}, u32[]{:S(2)}) collective-permute-start(bf16[64,8,128]{2,1,0:T(8,128)(2,1)S(1)} %collective-permute-done.4), channel_id=1, source_target_pairs={{0,1},{1,2},{2,3},{3,4},{4,5},{5,6},{6,7},{7,0},{8,9},{9,10},{10,1... | collective-permute-start | bytes 393224 | tf_op jit(solution)/shard_map/ppermute | solution.py:18
  30.5 17.9 %copy-start.5 = (bf16[1,512,128]{2,1,0:T(8,128)(2,1)S(1)}, bf16[1,512,128]{2,1,0:T(8,128)(2,1)}, u32[]{:S(2)}) copy-start(bf16[1,512,128]{2,1,0:T(8,128)(2,1)} %param.18) | copy-start | bytes 393220
  30.5 18.1 %copy-start.13 = (s32[64]{0:T(128)S(1)}, s32[64]{0:T(128)}, u32[]{:S(2)}) copy-start(s32[64]{0:T(128)} %param.20) | copy-start | bytes 772
  31.6 20.9 %copy-start.11 = (bf16[3,128]{1,0:T(4,128)(2,1)S(1)}, bf16[3,128]{1,0:T(4,128)(2,1)}, u32[]{:S(2)}) copy-start(bf16[3,128]{1,0:T(4,128)(2,1)} %param.23) | copy-start | bytes 2308
  31.6 20.9 %copy-start.6 = (bf16[1,512,128]{2,1,0:T(8,128)(2,1)S(1)}, bf16[1,512,128]{2,1,0:T(8,128)(2,1)}, u32[]{:S(2)}) copy-start(bf16[1,512,128]{2,1,0:T(8,128)(2,1)} %param.17) | copy-start | bytes 393220
  31.6 21.7 %copy-start.14 = (s32[64]{0:T(128)S(1)}, s32[64]{0:T(128)}, u32[]{:S(2)}) copy-start(s32[64]{0:T(128)} %param.19) | copy-start | bytes 772
  31.6 42.1 %all-to-all-start = ((bf16[64,8,1024]{2,1,0:T(8,128)(2,1)}), bf16[64,8,1024]{2,1,0:T(8,128)(2,1)S(1)}, u32[]{:S(2)}, u32[]{:S(2)}) async-start(bf16[64,8,1024]{2,1,0:T(8,128)(2,1)} %broadcast_select_fusion), calls=%async_computation | async-start | bytes 2097152 | tf_op jit(solution)/shard_map/all_to_all | solution.py:137
  48.4 99.3 %all-reduce.3.cloned.1.call-start = ((), (), s32[]{:S(2)}) async-start(), calls=%async_computation.2 | async-start | bytes 2097152 | tf_op jit(solution)/shard_map/psum | solution.py:156
  73.7 0.9 copy-start.3
  77.2 1.0 copy-start.4
  77.9 2.0 copy-start.9
  77.9 2.0 copy-start.12
  77.9 2.0 copy-start.7
  77.9 2.0 copy-start.8
  79.6 149.5 %all-reduce.5.cloned.1.call-start = ((), (), s32[]{:S(2)}) async-start(), calls=%async_computation.3 | async-start | bytes 2097152 | tf_op jit(solution)/shard_map/psum | solution.py:166
  147.6 1.7 copy-start.1
  150.6 5.7 %copy-start.10 = (bf16[1024]{0:T(1024)(128)(2,1)S(1)}, bf16[1024]{0:T(1024)(128)(2,1)}, u32[]{:S(2)}) copy-start(bf16[1024]{0:T(1024)(128)(2,1)} %param.31) | copy-start | bytes 6148
  150.6 5.9 %copy-start.15 = (s32[64]{0:T(128)S(1)}, s32[64]{0:T(128)}, u32[]{:S(2)}) copy-start(s32[64]{0:T(128)} %param.21) | copy-start | bytes 772
  229.1 1.7 copy-start.2
  234.5 25.1 %all-to-all-start.1 = ((bf16[64,2,512]{2,1,0:T(2,128)(2,1)}), bf16[64,2,512]{2,1,0:T(2,128)(2,1)S(1)}, u32[]{:S(2)}, u32[]{:S(2)}) async-start(bf16[64,2,512]{2,1,0:T(2,128)(2,1)} %reshape.238), calls=%async_computation.1 | async-start | bytes 262144 | tf_op jit(solution)/shard_map/all_to_all | solution.py:179
Sparse Core Ops, SparseCore 0:
  79.8 67.8 all-reduce.2
  156.4 72.6 all-reduce.4
